TPU v7x, 512 devices: a whole 4x8x8 slice. The times are simulated.
512 devices in a mesh: row: 4 (over z_hi), col: 16 (over z_lo, x, core), chan: 8 (over y).
Axes of the slice: x: 4, y: 8, z: 8 (z_hi: 4, z_lo: 2; z = z_hi * 2 + z_lo), core: 2. Of those that a mesh axis runs over, the one named last changes fastest.
Arguments:
- snapshots: bfloat16 [8192, 2048], P('col', 'chan'), may hold values from -45 to 45
- offsets: int32 [4], replicated, may hold values from 0 to 15
- window_len: int32 [8192], replicated, may hold values from 64 to 256, as said below
- cone_exp: int32 [8192], replicated, may hold values from 0 to 3
Outputs:
- kernel: float32 [2048, 8192], P(('row', 'chan'), 'col')
Inputs may be any that keep to these rules, and one draw needn't show every extreme that they name: `window_len`: each value is a lag window length; at least one snapshot has a window of 256 lags.
All inputs are finite; a program needn't handle non-finite values.
Results may differ from a plain program's by a relative error of at most 0.0003.
Values may be sent and summed in bfloat16 or wider, within the bound.
No kernel may reach another device: no remote copies, remote signals or barrier semaphores. Data moves between devices by JAX's collectives and lax.ppermute only.
A program may use at most 64 MiB of HBM per device.

v0:
```python
import jax
import jax.numpy as jnp
from jax import lax
from jax.sharding import PartitionSpec as P

C = 2048
LAGS = 256
epsilon = 1e-05


def shifted(block, axis, distance):
    devices = range(lax.axis_size(axis))
    route = [((i - distance) % len(devices), i) for i in devices]
    return lax.ppermute(block, axis, route)


def spread(value, axis, source):
    kept = jnp.where(lax.axis_index(axis) == source, value, 0).astype(value.dtype)
    return lax.psum(kept, axis)


def power_int(frac, exps):
    square = frac * frac
    return jnp.where(
        exps == 0,
        jnp.ones_like(frac),
        jnp.where(exps == 1, frac, jnp.where(exps == 2, square, square * frac)),
    )


def cone_matrix(lengths, exps, lags):
    rows = lengths.shape[0]
    row_pos = lax.broadcasted_iota(jnp.int32, (rows, rows + lags - 1), 0)
    col_pos = lax.broadcasted_iota(jnp.int32, (rows, rows + lags - 1), 1)
    lag = row_pos + (lags - 1) - col_pos
    span = lengths[:, None]
    valid = (lag >= 0) & (lag < span)
    frac = (span.astype(jnp.float32) - lag.astype(jnp.float32)) / span.astype(jnp.float32)
    cone = jnp.where(valid, power_int(frac, exps[:, None]), jnp.zeros_like(frac))
    return cone / jnp.sum(cone, axis=1, keepdims=True)


def lag_sum(weights, dist, count):
    depth = dist.shape[0]
    width = dist.shape[1]
    columns = width - (depth - count)
    padded = jnp.pad(dist, ((0, 0), (count - 1, 0)))
    stride = width + count - 1
    flat = jnp.pad(padded.reshape(-1), (0, depth))
    skewed = flat.reshape(depth, stride + 1)[:, : columns + count - 1]
    diagonal = jnp.dot(
        weights, skewed, precision=lax.Precision.HIGHEST, preferred_element_type=jnp.float32
    )
    lined = diagonal.reshape(-1)[count - 1 : count - 1 + count * (columns + count - 2)]
    return lined.reshape(count, columns + count - 2)[:, :columns]


def shards(snapshots, offsets, window_len, cone_exp):
    block = snapshots.shape[0]
    lags = LAGS
    tail = snapshots[block - (lags - 1) :]
    history = shifted(tail, "col", 1)
    col_ext = jnp.concatenate([history, snapshots], axis=0)
    chosen = lax.dynamic_index_in_dim(offsets, lax.axis_index("row"), 0, keepdims=False)
    row_ext = spread(col_ext, "col", chosen)
    row_begin = chosen * block
    col_begin = lax.axis_index("col") * block
    row_weights = cone_matrix(
        lax.dynamic_slice_in_dim(window_len, row_begin, block),
        lax.dynamic_slice_in_dim(cone_exp, row_begin, block),
        lags,
    )
    col_weights = cone_matrix(
        lax.dynamic_slice_in_dim(window_len, col_begin, block),
        lax.dynamic_slice_in_dim(cone_exp, col_begin, block),
        lags,
    )
    share = block // lax.axis_size("chan")
    first = lax.axis_index("chan") * share
    mine = lax.dynamic_slice(row_weights, (first, first), (share, share + lags - 1))
    row_wide = row_ext.astype(jnp.float32)
    col_wide = col_ext.astype(jnp.float32)
    row_part = jnp.sum(row_wide * row_wide, axis=1)
    col_part = jnp.sum(col_wide * col_wide, axis=1)
    inner = jnp.dot(row_ext, col_ext.T, preferred_element_type=jnp.float32)
    dist = row_part[:, None] + col_part[None, :] - 2.0 * inner
    total = lax.psum_scatter(
        lag_sum(row_weights, dist, lax.axis_size("chan") * share),
        "chan",
        scatter_dimension=0,
        tiled=True,
    )
    row_full, col_norms = lax.psum((row_part, col_part), "chan")
    row_near = lax.dynamic_slice_in_dim(row_full, first, share + lags - 1)
    row_scale = jnp.sqrt(
        jnp.dot(mine, row_near, precision=lax.Precision.HIGHEST, preferred_element_type=jnp.float32)
        / C
        + epsilon
    )
    col_scale = jnp.sqrt(
        jnp.dot(
            col_weights,
            col_norms,
            precision=lax.Precision.HIGHEST,
            preferred_element_type=jnp.float32,
        )
        / C
        + epsilon
    )
    return jnp.exp(-total / (2.0 * C * row_scale[:, None] * col_scale[None, :]))


def solution(mesh):
    in_specs = (P("col", "chan"), P(), P(), P())
    out_specs = P(("row", "chan"), "col")
    return jax.shard_map(shards, mesh=mesh, in_specs=in_specs, out_specs=out_specs, check_vma=False)
```

profile of v0, /device:TPU:2, one launch (start us, length us, event | category | flops | bytes accessed | tf_op | source)
XLA Modules:
  0.0 241.1 jit_solution(13446755895322598838)
XLA Ops:
  6.5 0.0 all-reduce.5.cloned.1.call-start
  6.5 1.0 slice.12
  7.5 1.9 collective-permute-start
  9.5 1.2 dynamic_slice.22
  11.4 0.8 dynamic-slice_compare_fusion.5
  12.8 0.8 fusion.31
  13.6 0.2 collective-permute-done
  13.8 1.8 broadcast_select_fusion
  15.6 0.0 all-reduce.5.cloned.1.call-update
  15.7 0.0 reduce-scatter.2.cloned.1.call-start
  15.7 2.5 %fusion.21 = (f32[512]{0:T(512)S(1)}, f32[512]{0:T(512)S(1)}) fusion(pred[512]{0:T(512)(128)(4,1)S(1)} %get-tuple-element.17, f32[512]{0:T(512)S(1)} %get-tuple-element.19, pred[512]{0:T(512)(128)(4,1)S(1)} %get-tuple-element.16, pred[512]{0:T(512)(128)(4,1)S(1)} %get-tuple-element.18, s32[512]{0:T(512)S(1)} %get-tuple-element.20, ...), kind=kLoop, calls=%fused_computation.28 | loop fusion | flops 9816576 | bytes 17408 | tf_op jit(solution)/shard_map/reduce_sum | solution.py:40
  18.2 0.2 multiply_reduce_fusion
  18.4 127.8 %all-reduce.5.cloned.1.call-done = bf16[767,256]{1,0:T(8,128)(2,1)} async-done(((bf16[767,256]{1,0:T(8,128)(2,1)}), bf16[767,256]{1,0:T(8,128)(2,1)}) %all-reduce.5.cloned.1.call-update) | async-done | bytes 392720 | tf_op jit(solution)/shard_map/psum | solution.py:19
  146.2 1.2 multiply_reduce_fusion.1
  147.4 1.5 multiply_subtract_fusion
  148.9 2.7 %pad.8 = f32[767,1278]{1,0:T(8,128)} pad(f32[767,767]{1,0:T(8,128)S(1)} %multiply_subtract_fusion, f32[]{:T(128)} %constant.14.clone.1), padding=0_0x511_0 | pad | bytes 6274064 | tf_op jit(solution)/shard_map/jit(_pad)/pad | solution.py:47
  151.7 5.5 %reshape.37 = f32[980226]{0:T(1024)} reshape(f32[767,1278]{1,0:T(8,128)} %pad.8) | data formatting | bytes 7841808 | tf_op jit(solution)/shard_map/reshape | solution.py:49
  157.1 4.3 %pad.9 = f32[980993]{0:T(1024)} pad(f32[980226]{0:T(1024)} %reshape.37, f32[]{:T(128)} %constant.14.clone.1), padding=0_767 | pad | bytes 7844880 | tf_op jit(solution)/shard_map/jit(_pad)/pad | solution.py:49
  161.4 7.8 %reshape.38 = f32[767,1279]{1,0:T(8,128)} reshape(f32[980993]{0:T(1024)} %pad.9) | data formatting | bytes 7847944 | tf_op jit(solution)/shard_map/reshape | solution.py:50
  169.2 9.2 %fusion = f32[512,1023]{1,0:T(8,128)} fusion(f32[767,1279]{1,0:T(8,128)} %reshape.38, f32[512]{0:T(512)S(1)} %get-tuple-element.6, pred[512]{0:T(512)(128)(4,1)S(1)} %get-tuple-element.15, f32[512]{0:T(512)S(1)} %get-tuple-element.9, pred[512]{0:T(512)(128)(4,1)S(1)} %get-tuple-element.14, pred[512]{0:T(512)(128)(4,1)S(1)} %get-tuple-element.13, ...), kind=kOutput, calls=%fused_computation | convolution fusion | flops 4826332160 | bytes 5250560 | tf_op jit(solution)/shard_map/dot_general | solution.py:51
  178.4 2.9 %reshape.39 = f32[523776]{0:T(1024)S(1)} reshape(f32[512,1023]{1,0:T(8,128)} %fusion) | data formatting | bytes 4190208 | tf_op jit(solution)/shard_map/reshape | solution.py:54
  181.4 2.0 slice.17
  183.3 3.4 %reshape.40 = f32[512,1022]{1,0:T(8,128)S(1)} reshape(f32[523264]{0:T(1024)} %slice.17) | data formatting | bytes 4186112 | tf_op jit(solution)/shard_map/reshape | solution.py:55
  186.7 1.1 slice.18
  187.8 0.0 reduce-scatter.2.cloned.1.call-update
  187.8 0.9 broadcast_divide_fusion
  188.7 16.4 %all-reduce.2 = (f32[767]{0:T(1024)S(1)}, f32[767]{0:T(1024)S(1)}) all-reduce(f32[767]{0:T(1024)S(1)} %multiply_reduce_fusion, f32[767]{0:T(1024)S(1)} %multiply_reduce_fusion.1), channel_id=1, replica_groups=mesh['row'=4,'col'=16,'chan'=8] {'chan'}, use_global_device_ids=true, to_apply=%region_7.8 | all-reduce | flops 1534 | bytes 12272 | tf_op jit(solution)/shard_map/psum | solution.py:93
  205.1 0.1 dynamic_slice.26
  205.2 0.3 fusion.18
  205.5 2.5 %fusion.13 = f32[1,512]{1,0:T(1,128)S(1)} fusion(f32[767,1]{0,1:T(1,128)S(1)} %reshape.43, f32[512]{0:T(512)S(1)} %get-tuple-element.5, f32[512]{0:T(512)S(1)} %get-tuple-element.19, s32[512]{0:T(512)S(1)} %get-tuple-element.20, s32[512]{0:T(512)S(1)} %get-tuple-element.21, pred[512]{0:T(512)(128)(4,1)S(1)} %get-tuple-element.17, ...), kind=kOutput, calls=%fused_computation.17 | convolution fusion | flops 10210304 | bytes 14844 | tf_op jit(solution)/shard_map/dot_general | solution.py:101
  208.0 24.6 %reduce-scatter.2.cloned.1.call-done = f32[64,512]{1,0:T(8,128)} async-done(((f32[512,512]{1,0:T(8,128)}), f32[64,512]{1,0:T(8,128)}) %reduce-scatter.2.cloned.1.call-update) | async-done | bytes 131088 | tf_op jit(solution)/shard_map/reduce_scatter | solution.py:87
  232.5 1.7 divide_exponential_fusion
  (5 shorter events, 0.0 us)
Async XLA Ops:
  6.5 11.7 %copy-start = (bf16[512,256]{1,0:T(8,128)(2,1)S(1)}, bf16[512,256]{1,0:T(8,128)(2,1)}, u32[]{:S(2)}) copy-start(bf16[512,256]{1,0:T(8,128)(2,1)} %param.4) | copy-start | bytes 786436
  6.5 139.7 %all-reduce.5.cloned.1.call-start = ((), (), s32[]{:S(2)}) async-start(), calls=%async_computation.1 | async-start | bytes 786432 | tf_op jit(solution)/shard_map/psum | solution.py:19
  7.5 6.3 %collective-permute-start = (bf16[255,256]{1,0:T(8,128)(2,1)S(1)}, bf16[255,256]{1,0:T(8,128)(2,1)S(1)}, u32[]{:S(2)}, u32[]{:S(2)}) collective-permute-start(bf16[255,256]{1,0:T(8,128)(2,1)S(1)} %slice.12), channel_id=1, source_target_pairs={{120,0},{0,8},{8,16},{16,24},{24,32},{32,40},{40,48},{48,56},{56,6... | collective-permute-start | bytes 391688 | tf_op jit(solution)/shard_map/ppermute | solution.py:14
  15.7 216.9 %reduce-scatter.2.cloned.1.call-start = ((), (), s32[]{:S(2)}) async-start(), calls=%async_computation.2 | async-start | bytes 1179648 | tf_op jit(solution)/shard_map/reduce_scatter | solution.py:87
Sparse Core Ops, SparseCore 0:
  15.8 130.3 all-reduce.4
  187.9 44.5 reduce-scatter.1
where the time goes:
time: 242 us; the launch traced here: 241 us
  waiting for transfers between devices  153 us (63%)
  local copies, waits for them, and re-layouts  32 us (13%)
  blocking collectives  16.4 us (7%)
  between operations  14.8 us (6%)
  matrix products  13.5 us (6%)
  other arithmetic  9.83 us (4%)
    psum x1, waiting for transfers between devices, spread(): return lax.psum(kept, axis)  128 us
    reduce_scatter x1, waiting for transfers between devices, shards(): lax.psum_scatter(lag_sum(row_weights, dist, lax.axis_size('chan') * share...  24.6 us
    psum x1, blocking collectives, shards(): row_full, col_norms = lax.psum((row_part, col_part), 'chan')  16.4 us
    dot_general x1, matrix products, lag_sum(): jnp.dot(weights, skewed, precision=lax.Precision.HIGHEST, preferred_eleme...  9.22 us
    reshape x1, local copies, waits for them, and re-layouts, lag_sum(): skewed = flat.reshape(depth, stride + 1)[:, :columns + count - 1]  7.81 us
    reshape x1, local copies, waits for them, and re-layouts, lag_sum(): flat = jnp.pad(padded.reshape(-1), (0, depth))  5.49 us
  transfers between devices with their start and end apart: 3, of which 3 were waited for; matrix products, arithmetic and copies ran while one was open for 4% of the time, Pallas kernels for 0%

commit v1 on v0

--- a/solution.py
+++ b/solution.py
@@ -8,6 +8,12 @@
 epsilon = 1e-05
 
 
+def add_all(block, mesh_axis):
+    pieces = lax.all_gather(block, mesh_axis, axis=0, tiled=False)
+    result = pieces.sum(axis=0)
+    return result
+
+
 def shifted(block, axis, distance):
     devices = range(lax.axis_size(axis))
     route = [((i - distance) % len(devices), i) for i in devices]
@@ -16,7 +22,7 @@
 
 def spread(value, axis, source):
     kept = jnp.where(lax.axis_index(axis) == source, value, 0).astype(value.dtype)
-    return lax.psum(kept, axis)
+    return add_all(kept, axis)
 
 
 def power_int(frac, exps):

time: 242 us -> 163 us (0.67)
  waiting for transfers between devices: 153 us -> 71 us
  other arithmetic: 9.83 us -> 12.7 us
    psum x1 -> x0, waiting for transfers between devices: 128 us -> none  [spread(): return lax.psum(kept, axis)]
    all_gather x0 -> x1, waiting for transfers between devices: none -> 47.3 us  [add_all(): pieces = lax.all_gather(block, mesh_axis, axis=0, tiled=False)]
    reduce_sum x0 -> x1, other arithmetic: none -> 3.85 us  [add_all(): result = pieces.sum(axis=0)]
    reduce_scatter x1, waiting for transfers between devices: 24.6 us -> 21.2 us  [shards(): lax.psum_scatter(lag_sum(row_weights, dist, lax.axis_size('chan') * share...]
  transfers between devices with their start and end apart: 3 -> 3, of which waited for: 3 -> 3; matrix products, arithmetic and copies ran while one was open for 4% -> 6% of each run, Pallas kernels for 0% -> 0%
where the time goes in v1:
time: 163 us; the launch traced here: 162 us
  waiting for transfers between devices  71 us (44%)
  local copies, waits for them, and re-layouts  32 us (20%)
  blocking collectives  17.2 us (11%)
  between operations  14.8 us (9%)
  other arithmetic  12.7 us (8%)
  matrix products  12.5 us (8%)
  starting transfers between devices  1.96 us (1%)
    all_gather x1, waiting for transfers between devices, add_all(): pieces = lax.all_gather(block, mesh_axis, axis=0, tiled=False)  47.3 us
    reduce_scatter x1, waiting for transfers between devices, shards(): lax.psum_scatter(lag_sum(row_weights, dist, lax.axis_size('chan') * share...  21.2 us
    psum x1, blocking collectives, shards(): row_full, col_norms = lax.psum((row_part, col_part), 'chan')  17.2 us
    dot_general x1, matrix products, lag_sum(): jnp.dot(weights, skewed, precision=lax.Precision.HIGHEST, preferred_eleme...  9.22 us
    reshape x1, local copies, waits for them, and re-layouts, lag_sum(): skewed = flat.reshape(depth, stride + 1)[:, :columns + count - 1]  7.81 us
    reshape x1, local copies, waits for them, and re-layouts, lag_sum(): flat = jnp.pad(padded.reshape(-1), (0, depth))  5.49 us
    pad x1, local copies, waits for them, and re-layouts, lag_sum(): flat = jnp.pad(padded.reshape(-1), (0, depth))  4.26 us
    reduce_sum x1, other arithmetic, add_all(): result = pieces.sum(axis=0)  3.85 us
  transfers between devices with their start and end apart: 3, of which 3 were waited for; matrix products, arithmetic and copies ran while one was open for 6% of the time, Pallas kernels for 0%

profile of v1, /device:TPU:2, one launch (start us, length us, event | category | flops | bytes accessed | tf_op | source)
XLA Modules:
  0.0 162.1 jit_solution(15728369632697735857)
XLA Ops:
  6.5 1.0 slice.12
  7.5 1.9 %collective-permute-start = (bf16[255,256]{1,0:T(8,128)(2,1)S(1)}, bf16[255,256]{1,0:T(8,128)(2,1)S(1)}, u32[]{:S(2)}, u32[]{:S(2)}) collective-permute-start(bf16[255,256]{1,0:T(8,128)(2,1)S(1)} %slice.12), channel_id=1, source_target_pairs={{120,0},{0,8},{8,16},{16,24},{24,32},{32,40},{40,48},{48,56},{56,6... | collective-permute-start | bytes 391688 | tf_op jit(solution)/shard_map/ppermute | solution.py:20
  9.5 1.2 dynamic_slice.22
  11.4 2.5 %collective-permute-done = bf16[255,256]{1,0:T(8,128)(2,1)S(1)} collective-permute-done((bf16[255,256]{1,0:T(8,128)(2,1)S(1)}, bf16[255,256]{1,0:T(8,128)(2,1)S(1)}, u32[]{:S(2)}, u32[]{:S(2)}) %collective-permute-start) | collective-permute-done | bytes 130592 | tf_op jit(solution)/shard_map/ppermute | solution.py:20
  13.8 1.8 %maximum_select_fusion = bf16[1,767,256]{2,1,0:T(8,128)(2,1)} fusion(bf16[1,512,256]{2,1,0:T(8,128)(2,1)} %bitcast.17, bf16[1,255,256]{2,1,0:T(8,128)(2,1)S(1)} %bitcast.18, pred[]{:T(512)S(6)} %eq.30), kind=kLoop, calls=%fused_computation.30 | loop fusion | flops 981760 | bytes 785409 | tf_op jit(solution)/shard_map/jit(_where)/select_n | solution.py:24
  15.7 0.0 all-gather.2.cloned.1.call-update
  15.7 0.0 reduce-scatter.2.cloned.1.call-start
  16.4 0.8 dynamic-slice_compare_fusion.5
  17.2 0.8 fusion.31
  18.0 2.5 %fusion.21 = (f32[512]{0:T(512)S(1)}, f32[512]{0:T(512)S(1)}) fusion(pred[512]{0:T(512)(128)(4,1)S(1)} %get-tuple-element.17, f32[512]{0:T(512)S(1)} %get-tuple-element.19, pred[512]{0:T(512)(128)(4,1)S(1)} %get-tuple-element.16, pred[512]{0:T(512)(128)(4,1)S(1)} %get-tuple-element.18, s32[512]{0:T(512)S(1)} %get-tuple-element.20, ...), kind=kLoop, calls=%fused_computation.28 | loop fusion | flops 9816576 | bytes 17408 | tf_op jit(solution)/shard_map/reduce_sum | solution.py:46
  20.4 0.2 multiply_reduce_fusion
  20.6 47.3 %all-gather.2.cloned.1.call-done = bf16[16,767,256]{2,1,0:T(8,128)(2,1)} async-done(((bf16[1,767,256]{2,1,0:T(8,128)(2,1)}), bf16[16,767,256]{2,1,0:T(8,128)(2,1)}) %all-gather.2.cloned.1.call-update) | async-done | bytes 6283280 | tf_op jit(solution)/shard_map/all_gather | solution.py:12
  68.0 3.9 %reduce_sum.49 = bf16[767,256]{1,0:T(8,128)(2,1)S(1)} reduce(bf16[16,767,256]{2,1,0:T(8,128)(2,1)} %all-gather.2.cloned.1.call-done, bf16[]{:T(256)} %constant.17.clone.1), dimensions={0}, to_apply=%region_1.2 | reduce | flops 2945280 | bytes 6675970 | tf_op jit(solution)/shard_map/reduce_sum | solution.py:13
  71.8 0.2 multiply_reduce_fusion.1
  72.0 0.5 multiply_subtract_fusion
  72.5 2.7 %pad.8 = f32[767,1278]{1,0:T(8,128)} pad(f32[767,767]{1,0:T(8,128)S(1)} %multiply_subtract_fusion, f32[]{:T(128)} %constant.15.clone.1), padding=0_0x511_0 | pad | bytes 6274064 | tf_op jit(solution)/shard_map/jit(_pad)/pad | solution.py:53
  75.3 5.5 %reshape.66 = f32[980226]{0:T(1024)} reshape(f32[767,1278]{1,0:T(8,128)} %pad.8) | data formatting | bytes 7841808 | tf_op jit(solution)/shard_map/reshape | solution.py:55
  80.8 4.3 %pad.9 = f32[980993]{0:T(1024)} pad(f32[980226]{0:T(1024)} %reshape.66, f32[]{:T(128)} %constant.15.clone.1), padding=0_767 | pad | bytes 7844880 | tf_op jit(solution)/shard_map/jit(_pad)/pad | solution.py:55
  85.0 7.8 %reshape.67 = f32[767,1279]{1,0:T(8,128)} reshape(f32[980993]{0:T(1024)} %pad.9) | data formatting | bytes 7847944 | tf_op jit(solution)/shard_map/reshape | solution.py:56
  92.8 9.2 %fusion = f32[512,1023]{1,0:T(8,128)} fusion(f32[767,1279]{1,0:T(8,128)} %reshape.67, f32[512]{0:T(512)S(1)} %get-tuple-element.6, pred[512]{0:T(512)(128)(4,1)S(1)} %get-tuple-element.15, f32[512]{0:T(512)S(1)} %get-tuple-element.9, pred[512]{0:T(512)(128)(4,1)S(1)} %get-tuple-element.14, pred[512]{0:T(512)(128)(4,1)S(1)} %get-tuple-element.13, ...), kind=kOutput, calls=%fused_computation | convolution fusion | flops 4826332160 | bytes 5250560 | tf_op jit(solution)/shard_map/dot_general | solution.py:57
  102.1 2.9 %reshape.68 = f32[523776]{0:T(1024)S(1)} reshape(f32[512,1023]{1,0:T(8,128)} %fusion) | data formatting | bytes 4190208 | tf_op jit(solution)/shard_map/reshape | solution.py:60
  105.0 2.0 %slice.17 = f32[523264]{0:T(1024)} slice(f32[523776]{0:T(1024)S(1)} %reshape.68), slice={[511:523775]} | slice | bytes 4186112 | tf_op jit(solution)/shard_map/slice | solution.py:60
  106.9 3.4 %reshape.69 = f32[512,1022]{1,0:T(8,128)S(1)} reshape(f32[523264]{0:T(1024)} %slice.17) | data formatting | bytes 4186112 | tf_op jit(solution)/shard_map/reshape | solution.py:61
  110.3 1.1 slice.18
  111.4 0.0 reduce-scatter.2.cloned.1.call-update
  111.4 0.9 broadcast_divide_fusion
  112.3 17.2 %all-reduce.2 = (f32[767]{0:T(1024)S(1)}, f32[767]{0:T(1024)S(1)}) all-reduce(f32[767]{0:T(1024)S(1)} %multiply_reduce_fusion, f32[767]{0:T(1024)S(1)} %multiply_reduce_fusion.1), channel_id=1, replica_groups=mesh['row'=4,'col'=16,'chan'=8] {'chan'}, use_global_device_ids=true, to_apply=%region_7.8 | all-reduce | flops 1534 | bytes 12272 | tf_op jit(solution)/shard_map/psum | solution.py:99
  129.6 0.1 dynamic_slice.26
  129.7 0.3 fusion.18
  129.9 2.5 %fusion.13 = f32[1,512]{1,0:T(1,128)S(1)} fusion(f32[767,1]{0,1:T(1,128)S(1)} %reshape.72, f32[512]{0:T(512)S(1)} %get-tuple-element.5, f32[512]{0:T(512)S(1)} %get-tuple-element.19, s32[512]{0:T(512)S(1)} %get-tuple-element.20, s32[512]{0:T(512)S(1)} %get-tuple-element.21, pred[512]{0:T(512)(128)(4,1)S(1)} %get-tuple-element.17, ...), kind=kOutput, calls=%fused_computation.17 | convolution fusion | flops 10210304 | bytes 14844 | tf_op jit(solution)/shard_map/dot_general | solution.py:107
  132.4 21.2 %reduce-scatter.2.cloned.1.call-done = f32[64,512]{1,0:T(8,128)} async-done(((f32[512,512]{1,0:T(8,128)}), f32[64,512]{1,0:T(8,128)}) %reduce-scatter.2.cloned.1.call-update) | async-done | bytes 131088 | tf_op jit(solution)/shard_map/reduce_scatter | solution.py:93
  153.6 1.7 %divide_exponential_fusion = f32[64,512]{1,0:T(8,128)} fusion(f32[64,512]{1,0:T(8,128)} %reduce-scatter.2.cloned.1.call-done, f32[512]{0:T(512)S(1)} %add_sqrt_fusion, f32[64]{0:T(128)S(1)} %fusion.18), kind=kLoop, calls=%fused_computation.32 | loop fusion | flops 98304 | bytes 264448 | tf_op jit(solution)/shard_map/exp | solution.py:116
  (6 shorter events, 0.0 us)
Async XLA Ops:
  6.5 13.9 %copy-start = (bf16[512,256]{1,0:T(8,128)(2,1)S(1)}, bf16[512,256]{1,0:T(8,128)(2,1)}, u32[]{:S(2)}) copy-start(bf16[512,256]{1,0:T(8,128)(2,1)} %param.4) | copy-start | bytes 786436
  6.5 61.4 %all-gather.2.cloned.1.call-start = ((), (), s32[]{:S(2)}) async-start(), calls=%async_computation.1 | async-start | bytes 6684672 | tf_op jit(solution)/shard_map/all_gather | solution.py:12
  7.5 6.3 %collective-permute-start = (bf16[255,256]{1,0:T(8,128)(2,1)S(1)}, bf16[255,256]{1,0:T(8,128)(2,1)S(1)}, u32[]{:S(2)}, u32[]{:S(2)}) collective-permute-start(bf16[255,256]{1,0:T(8,128)(2,1)S(1)} %slice.12), channel_id=1, source_target_pairs={{120,0},{0,8},{8,16},{16,24},{24,32},{32,40},{40,48},{48,56},{56,6... | collective-permute-start | bytes 391688 | tf_op jit(solution)/shard_map/ppermute | solution.py:20
  15.7 137.9 %reduce-scatter.2.cloned.1.call-start = ((), (), s32[]{:S(2)}) async-start(), calls=%async_computation.2 | async-start | bytes 1179648 | tf_op jit(solution)/shard_map/reduce_scatter | solution.py:93
Sparse Core Ops, SparseCore 0:
  15.8 52.1 all-gather.1
  111.5 42.0 reduce-scatter.1
